TPU v7x, 32 devices: a whole 2x2x4 slice. The times are simulated.
32 devices in a mesh: row: 4 (over z), col: 8 (over y, x, core).
Axes of the slice: x: 2, y: 2, z: 4, core: 2. Of those that a mesh axis runs over, the one named last changes fastest.
Arguments:
- image: float32 [224, 32, 2048], P(None, 'row', 'col'), may hold values from -24 to 24
- start_basis: float32 [224, 16], replicated, may hold values from -4 to 4
Outputs:
- smoothed: float32 [224, 32, 2048], P(None, 'row', 'col')
- lowrank: float32 [224, 32, 2048], P(None, 'row', 'col')
All inputs are finite; a program needn't handle non-finite values.
Results may differ from a plain program's by a relative error of at most 0.0003.
Values sent between devices are 32-bit elements; how exact they have to be, the bound alone decides.
No kernel may reach another device: no remote copies, remote signals or barrier semaphores. Data moves between devices by JAX's collectives and lax.ppermute only.
A program may use at most 64 MiB of HBM per device.

v0:
```python
import jax
import jax.numpy as jnp
from jax import lax
from jax.sharding import PartitionSpec as P

SWEEPS = 4
SUBIT = 2
tau_step = 0.22
fidelity = 0.1


def padded_2(cells, sides, width):
    for axis, dim in sides:
        count = lax.axis_size(axis)
        ends = count - 1
        head = lax.slice_in_dim(cells, 0, width, axis=dim)
        tail = lax.slice_in_dim(cells, cells.shape[dim] - width, cells.shape[dim], axis=dim)
        cells = jnp.concatenate(
            [
                lax.ppermute(tail, axis, [(i, (i + 1) % count) for i in range(ends)]),
                cells,
                lax.ppermute(head, axis, [((i + 1) % count, i) for i in range(ends)]),
            ],
            axis=dim,
        )
    return cells


def forward_diffs(padded):
    diff_col = padded[..., :-1, 1:] - padded[..., :-1, :-1]
    diff_row = padded[..., 1:, :-1] - padded[..., :-1, :-1]
    return (diff_col, diff_row)


def smooth_step(padded, source):
    diff_col, diff_row = forward_diffs(padded)
    energy_sum = jnp.sum(diff_col * diff_col + diff_row * diff_row, axis=0)
    weight = 1.0 / jnp.sqrt(1.0 + energy_sum / padded.shape[0])
    flux_col = weight * diff_col
    flux_row = weight * diff_row
    spread = (
        flux_col[..., 1:, 1:]
        - flux_col[..., 1:, :-1]
        + flux_row[..., 1:, 1:]
        - flux_row[..., :-1, 1:]
    )
    centre = padded[..., 1:-1, 1:-1]
    return centre + tau_step * spread + tau_step * fidelity * (source - centre)


def orthonormal(block):
    inner = jnp.dot(block.T, block, precision=lax.Precision.HIGHEST)
    lower = jnp.linalg.cholesky(inner)
    return lax.linalg.triangular_solve(lower, block, left_side=False, lower=True, transpose_a=True)


def shards(image, start_basis):
    band_count, tile_rows, tile_cols = image.shape
    field = image
    for sweep_no in range(SWEEPS):
        extended = padded_2(field, (("row", 1), ("col", 2)), 1)
        field = smooth_step(extended, image)
    flat_field = field.reshape(band_count, tile_rows * tile_cols)
    basis_now = start_basis
    local_gram = lax.dot_general(
        flat_field,
        flat_field,
        (((1,), (1,)), ((), ())),
        precision=lax.Precision.HIGHEST,
        preferred_element_type=jnp.float32,
    )
    gram_full = lax.psum(local_gram, ("row", "col"))
    for turn in range(SUBIT):
        product = jnp.dot(gram_full, basis_now, precision=lax.Precision.HIGHEST)
        basis_now = orthonormal(orthonormal(product))
    coeffs = jnp.dot(basis_now.T, flat_field, precision=lax.Precision.HIGHEST)
    lowrank = jnp.dot(basis_now, coeffs, precision=lax.Precision.HIGHEST)
    return (field, lowrank.reshape(band_count, tile_rows, tile_cols))


def solution(mesh):
    in_specs = (P(None, "row", "col"), P())
    out_specs = (P(None, "row", "col"), P(None, "row", "col"))
    return jax.shard_map(shards, mesh=mesh, in_specs=in_specs, out_specs=out_specs, check_vma=False)
```

profile of v0, /device:TPU:1, one launch (start us, length us, event | category | flops | bytes accessed | tf_op | source)
XLA Modules:
  0.0 325.3 jit_solution(15934660971049037170)
XLA Ops:
  7.2 2.4 fusion.42
  9.6 1.3 collective-permute-start.1
  10.9 4.7 %collective-permute-start = (f32[224,1,256]{2,0,1:T(8,128)S(1)}, f32[224,1,256]{2,0,1:T(8,128)S(1)}, u32[]{:S(2)}, u32[]{:S(2)}) collective-permute-start(f32[224,1,256]{2,0,1:T(8,128)S(1)} %copy.216), channel_id=1, source_target_pairs={{0,8},{8,16},{16,24},{1,9},{9,17},{17,25},{2,10},{10,18},{18,26},{... | collective-permute-start | bytes 688136 | tf_op jit(solution)/shard_map/ppermute | solution.py:20
  15.6 2.2 copy.184
  17.9 1.1 collective-permute-done.1
  20.0 4.7 %collective-permute-start.3 = (f32[224,10,1]{0,1,2:T(8,128)S(1)}, f32[224,10,1]{0,1,2:T(8,128)S(1)}, u32[]{:S(2)}, u32[]{:S(2)}) collective-permute-start(f32[224,10,1]{0,1,2:T(8,128)S(1)} %get-tuple-element.29), channel_id=1, source_target_pairs={{0,1},{1,2},{2,3},{3,4},{4,5},{5,6},{6,7},{8,9},{9,10},{10,11},{11... | collective-permute-start | bytes 26888 | tf_op jit(solution)/shard_map/ppermute | solution.py:20
  24.8 1.9 collective-permute-start.2
  27.6 2.3 collective-permute-done.2
  29.8 2.7 add_reduce_fusion.3
  32.8 6.5 %broadcast_multiply_fusion.7 = (f32[224,9,257]{0,1,2:T(8,128)S(1)}, f32[224,9,257]{0,1,2:T(8,128)S(1)}) fusion(f32[9,257]{0,1:T(8,128)S(1)} %copy.183, f32[224,10,257]{0,1,2:T(8,128)} %copy-done.1, f32[224,10,1]{0,1,2:T(8,128)S(1)} %collective-permute-done.2, f32[224,1,256]{0,1,2:T(1,128)S(1)} %copy.181, f32[224,8,256]{0,1,2:T(8,128)S(1)} %copy.184, ...), kind=kLoop, calls=%fused_computation.35 | loop fusion | flops 3626784 | bytes 10601764 | tf_op jit(solution)/shard_map/mul | solution.py:39
  40.3 1.3 copy-done.11
  42.1 1.3 collective-permute-start.5
  43.6 4.7 %collective-permute-start.4 = (f32[224,1,256]{2,0,1:T(8,128)S(1)}, f32[224,1,256]{2,0,1:T(8,128)S(1)}, u32[]{:S(2)}, u32[]{:S(2)}) collective-permute-start(f32[224,1,256]{2,0,1:T(8,128)S(1)} %copy.187), channel_id=1, source_target_pairs={{0,8},{8,16},{16,24},{1,9},{9,17},{17,25},{2,10},{10,18},{18,26},{... | collective-permute-start | bytes 688136 | tf_op jit(solution)/shard_map/ppermute | solution.py:20
  48.3 2.0 collective-permute-done.5
  50.5 1.7 collective-permute-done.4
  53.3 5.5 %collective-permute-start.7 = (f32[224,10,1]{0,1,2:T(8,128)S(1)}, f32[224,10,1]{0,1,2:T(8,128)S(1)}, u32[]{:S(2)}, u32[]{:S(2)}) collective-permute-start(f32[224,10,1]{0,1,2:T(8,128)S(1)} %get-tuple-element.27), channel_id=1, source_target_pairs={{0,1},{1,2},{2,3},{3,4},{4,5},{5,6},{6,7},{8,9},{9,10},{10,11},{11... | collective-permute-start | bytes 26888 | tf_op jit(solution)/shard_map/ppermute | solution.py:20
  58.8 2.1 collective-permute-start.6
  60.9 2.4 maximum_maximum_fusion.1
  63.9 1.5 copy-done.2
  65.3 2.8 add_reduce_fusion.2
  68.4 8.4 %broadcast_multiply_fusion.5 = (f32[224,9,257]{0,1,2:T(8,128)S(1)}, f32[224,9,257]{0,1,2:T(8,128)}) fusion(f32[9,257]{0,1:T(8,128)S(1)} %copy.192, f32[224,10,257]{0,1,2:T(8,128)} %copy-done.2, f32[224,10,1]{0,1,2:T(8,128)S(1)} %collective-permute-done.6, f32[224,1,256]{0,1,2:T(1,128)S(1)} %copy.190, f32[224,8,256]{0,1,2:T(8,128)} %copy-done.11, ...), kind=kLoop, calls=%fused_computation.33 | loop fusion | flops 3626784 | bytes 10601764 | tf_op jit(solution)/shard_map/mul | solution.py:39
  76.7 3.8 %fusion.12 = f32[224,8,256]{0,1,2:T(8,128)S(1)} fusion(f32[224,8,256]{0,1,2:T(8,128)S(1)} %copy-done.13, f32[224,9,257]{0,1,2:T(8,128)} %get-tuple-element.19, f32[224,9,257]{0,1,2:T(8,128)S(1)} %get-tuple-element.18, f32[224,8,256]{0,1,2:T(8,128)S(1)} %copy.184), kind=kLoop, calls=%fused_computation.51 | loop fusion | flops 3670016 | bytes 12845056 | tf_op jit(solution)/shard_map/add | solution.py:48
  80.6 1.3 copy-done.8
  82.4 1.3 collective-permute-start.9
  83.8 4.7 %collective-permute-start.8 = (f32[224,1,256]{2,0,1:T(8,128)S(1)}, f32[224,1,256]{2,0,1:T(8,128)S(1)}, u32[]{:S(2)}, u32[]{:S(2)}) collective-permute-start(f32[224,1,256]{2,0,1:T(8,128)S(1)} %copy.194), channel_id=1, source_target_pairs={{0,8},{8,16},{16,24},{1,9},{9,17},{17,25},{2,10},{10,18},{18,26},{... | collective-permute-start | bytes 688136 | tf_op jit(solution)/shard_map/ppermute | solution.py:20
  88.6 1.3 collective-permute-done.9
  90.1 1.5 collective-permute-done.8
  92.6 5.2 %collective-permute-start.11 = (f32[224,10,1]{0,1,2:T(8,128)S(1)}, f32[224,10,1]{0,1,2:T(8,128)S(1)}, u32[]{:S(2)}, u32[]{:S(2)}) collective-permute-start(f32[224,10,1]{0,1,2:T(8,128)S(1)} %get-tuple-element.25), channel_id=1, source_target_pairs={{0,1},{1,2},{2,3},{3,4},{4,5},{5,6},{6,7},{8,9},{9,10},{10,11},{11... | collective-permute-start | bytes 26888 | tf_op jit(solution)/shard_map/ppermute | solution.py:20
  97.8 1.9 collective-permute-start.10
  99.7 2.4 maximum_maximum_fusion.2
  102.9 1.3 copy-done.3
  104.1 2.8 add_reduce_fusion.1
  107.2 8.4 %broadcast_multiply_fusion.3 = (f32[224,9,257]{0,1,2:T(8,128)S(1)}, f32[224,9,257]{0,1,2:T(8,128)}) fusion(f32[9,257]{0,1:T(8,128)S(1)} %copy.199, f32[224,10,257]{0,1,2:T(8,128)} %copy-done.3, f32[224,10,1]{0,1,2:T(8,128)S(1)} %collective-permute-done.10, f32[224,1,256]{0,1,2:T(1,128)S(1)} %copy.197, f32[224,8,256]{0,1,2:T(8,128)} %copy-done.8, ...), kind=kLoop, calls=%fused_computation.31 | loop fusion | flops 3626784 | bytes 10601764 | tf_op jit(solution)/shard_map/mul | solution.py:39
  115.5 3.8 %fusion.9 = f32[224,8,256]{0,1,2:T(8,128)S(1)} fusion(f32[224,8,256]{0,1,2:T(8,128)S(1)} %copy-done.10, f32[224,9,257]{0,1,2:T(8,128)} %get-tuple-element.17, f32[224,9,257]{0,1,2:T(8,128)S(1)} %get-tuple-element.16, f32[224,8,256]{0,1,2:T(8,128)S(1)} %copy.184), kind=kLoop, calls=%fused_computation.45 | loop fusion | flops 3670016 | bytes 12845056 | tf_op jit(solution)/shard_map/add | solution.py:48
  119.4 1.3 copy-done.5
  121.2 1.3 collective-permute-start.13
  122.6 5.0 %collective-permute-start.12 = (f32[224,1,256]{2,0,1:T(8,128)S(1)}, f32[224,1,256]{2,0,1:T(8,128)S(1)}, u32[]{:S(2)}, u32[]{:S(2)}) collective-permute-start(f32[224,1,256]{2,0,1:T(8,128)S(1)} %copy.201), channel_id=1, source_target_pairs={{0,8},{8,16},{16,24},{1,9},{9,17},{17,25},{2,10},{10,18},{18,26},{... | collective-permute-start | bytes 688136 | tf_op jit(solution)/shard_map/ppermute | solution.py:20
  127.6 1.1 collective-permute-done.13
  128.9 1.5 collective-permute-done.12
  131.4 5.4 %collective-permute-start.15 = (f32[224,10,1]{0,1,2:T(8,128)S(1)}, f32[224,10,1]{0,1,2:T(8,128)S(1)}, u32[]{:S(2)}, u32[]{:S(2)}) collective-permute-start(f32[224,10,1]{0,1,2:T(8,128)S(1)} %get-tuple-element.23), channel_id=1, source_target_pairs={{0,1},{1,2},{2,3},{3,4},{4,5},{5,6},{6,7},{8,9},{9,10},{10,11},{11... | collective-permute-start | bytes 26888 | tf_op jit(solution)/shard_map/ppermute | solution.py:20
  136.8 1.9 collective-permute-start.14
  138.7 2.4 maximum_maximum_fusion.3
  141.8 1.3 copy-done.4
  143.1 2.8 add_reduce_fusion
  146.1 8.4 %broadcast_multiply_fusion.1 = (f32[224,9,257]{0,1,2:T(8,128)S(1)}, f32[224,9,257]{0,1,2:T(8,128)}) fusion(f32[9,257]{0,1:T(8,128)S(1)} %copy.206, f32[224,10,257]{0,1,2:T(8,128)} %copy-done.4, f32[224,10,1]{0,1,2:T(8,128)S(1)} %collective-permute-done.14, f32[224,1,256]{0,1,2:T(1,128)S(1)} %copy.204, f32[224,8,256]{0,1,2:T(8,128)} %copy-done.5, ...), kind=kLoop, calls=%fused_computation.29 | loop fusion | flops 3626784 | bytes 10601764 | tf_op jit(solution)/shard_map/mul | solution.py:39
  154.5 3.8 %fusion.6 = f32[224,8,256]{0,1,2:T(8,128)S(1)} fusion(f32[224,8,256]{0,1,2:T(8,128)S(1)} %copy-done.7, f32[224,9,257]{0,1,2:T(8,128)} %get-tuple-element.15, f32[224,9,257]{0,1,2:T(8,128)S(1)} %get-tuple-element.14, f32[224,8,256]{0,1,2:T(8,128)S(1)} %copy.184), kind=kLoop, calls=%fused_computation.39 | loop fusion | flops 3670016 | bytes 12845056 | tf_op jit(solution)/shard_map/add | solution.py:48
  158.3 1.3 copy-done.14
  159.7 5.0 %fusion.18 = f32[224,224]{1,0:T(8,128)} fusion(f32[224,8,256]{0,1,2:T(8,128)S(1)} %fusion.6), kind=kOutput, calls=%fused_computation.62 | convolution fusion | flops 1233125376 | bytes 2035712 | tf_op jit(solution)/shard_map/dot_general | solution.py:65
  164.7 2.6 copy.215
  167.3 2.0 copy.218
  169.3 122.3 %all-reduce.2.cloned.1.call-done = f32[224,224]{1,0:T(8,128)} async-done(((f32[224,224]{1,0:T(8,128)}), f32[224,224]{1,0:T(8,128)}) %all-reduce.2.cloned.1.call-update) | async-done | bytes 200720 | tf_op jit(solution)/shard_map/psum | solution.py:72
  291.6 1.2 fusion.43
  293.1 1.5 cholesky.74
  296.0 1.2 custom-call.8
  297.6 1.5 cholesky.85
  300.6 1.2 custom-call.9
  302.0 1.2 fusion.46
  303.5 1.5 cholesky.96
  306.4 1.2 custom-call.10
  308.0 1.5 cholesky.107
  310.9 1.2 custom-call.11
  312.4 2.5 fusion.49
  314.9 1.6 fusion.50
  316.5 2.0 copy.219
  (100 shorter events, 18.6 us)
Async XLA Ops:
  7.2 284.4 %copy-start = (f32[224,16]{0,1:T(8,128)S(1)}, f32[224,16]{0,1:T(8,128)}, u32[]{:S(2)}) copy-start(f32[224,16]{0,1:T(8,128)} %param.6) | copy-start | bytes 43012
  7.2 284.4 %all-reduce.2.cloned.1.call-start = ((), (), s32[]{:S(2)}) async-start(), calls=%async_computation | async-start | bytes 458752 | tf_op jit(solution)/shard_map/psum | solution.py:72
  9.6 9.4 %collective-permute-start.1 = (f32[224,1,256]{2,0,1:T(8,128)S(1)}, f32[224,1,256]{2,0,1:T(8,128)S(1)}, u32[]{:S(2)}, u32[]{:S(2)}) collective-permute-start(f32[224,1,256]{2,0,1:T(8,128)S(1)} %copy.217), channel_id=1, source_target_pairs={{8,0},{16,8},{24,16},{9,1},{17,9},{25,17},{10,2},{18,10},{26,18},{... | collective-permute-start | bytes 688136 | tf_op jit(solution)/shard_map/ppermute | solution.py:22
  10.9 8.9 %collective-permute-start = (f32[224,1,256]{2,0,1:T(8,128)S(1)}, f32[224,1,256]{2,0,1:T(8,128)S(1)}, u32[]{:S(2)}, u32[]{:S(2)}) collective-permute-start(f32[224,1,256]{2,0,1:T(8,128)S(1)} %copy.216), channel_id=1, source_target_pairs={{0,8},{8,16},{16,24},{1,9},{9,17},{17,25},{2,10},{10,18},{18,26},{... | collective-permute-start | bytes 688136 | tf_op jit(solution)/shard_map/ppermute | solution.py:20
  20.0 6.6 %collective-permute-start.3 = (f32[224,10,1]{0,1,2:T(8,128)S(1)}, f32[224,10,1]{0,1,2:T(8,128)S(1)}, u32[]{:S(2)}, u32[]{:S(2)}) collective-permute-start(f32[224,10,1]{0,1,2:T(8,128)S(1)} %get-tuple-element.29), channel_id=1, source_target_pairs={{0,1},{1,2},{2,3},{3,4},{4,5},{5,6},{6,7},{8,9},{9,10},{10,11},{11... | collective-permute-start | bytes 26888 | tf_op jit(solution)/shard_map/ppermute | solution.py:20
  24.8 5.1 %collective-permute-start.2 = (f32[224,10,1]{0,1,2:T(8,128)S(1)}, f32[224,10,1]{0,1,2:T(8,128)S(1)}, u32[]{:S(2)}, u32[]{:S(2)}) collective-permute-start(f32[224,10,1]{0,1,2:T(8,128)S(1)} %get-tuple-element.28), channel_id=1, source_target_pairs={{1,0},{2,1},{3,2},{4,3},{5,4},{6,5},{7,6},{9,8},{10,9},{11,10},{12... | collective-permute-start | bytes 26888 | tf_op jit(solution)/shard_map/ppermute | solution.py:22
  27.5 2.3 copy-start.1
  40.3 1.4 copy-start.11
  42.1 8.2 %collective-permute-start.5 = (f32[224,1,256]{2,0,1:T(8,128)S(1)}, f32[224,1,256]{2,0,1:T(8,128)S(1)}, u32[]{:S(2)}, u32[]{:S(2)}) collective-permute-start(f32[224,1,256]{2,0,1:T(8,128)S(1)} %copy.188), channel_id=1, source_target_pairs={{8,0},{16,8},{24,16},{9,1},{17,9},{25,17},{10,2},{18,10},{26,18},{... | collective-permute-start | bytes 688136 | tf_op jit(solution)/shard_map/ppermute | solution.py:22
  43.6 8.6 %collective-permute-start.4 = (f32[224,1,256]{2,0,1:T(8,128)S(1)}, f32[224,1,256]{2,0,1:T(8,128)S(1)}, u32[]{:S(2)}, u32[]{:S(2)}) collective-permute-start(f32[224,1,256]{2,0,1:T(8,128)S(1)} %copy.187), channel_id=1, source_target_pairs={{0,8},{8,16},{16,24},{1,9},{9,17},{17,25},{2,10},{10,18},{18,26},{... | collective-permute-start | bytes 688136 | tf_op jit(solution)/shard_map/ppermute | solution.py:20
  52.4 13.0 %copy-start.12 = (f32[224,8,256]{0,1,2:T(8,128)S(1)}, f32[224,8,256]{0,1,2:T(8,128)}, u32[]{:S(2)}) copy-start(f32[224,8,256]{0,1,2:T(8,128)} %copy-done.11) | copy-start | bytes 5505028
  53.3 7.7 %collective-permute-start.7 = (f32[224,10,1]{0,1,2:T(8,128)S(1)}, f32[224,10,1]{0,1,2:T(8,128)S(1)}, u32[]{:S(2)}, u32[]{:S(2)}) collective-permute-start(f32[224,10,1]{0,1,2:T(8,128)S(1)} %get-tuple-element.27), channel_id=1, source_target_pairs={{0,1},{1,2},{2,3},{3,4},{4,5},{5,6},{6,7},{8,9},{9,10},{10,11},{11... | collective-permute-start | bytes 26888 | tf_op jit(solution)/shard_map/ppermute | solution.py:20
  58.8 5.1 %collective-permute-start.6 = (f32[224,10,1]{0,1,2:T(8,128)S(1)}, f32[224,10,1]{0,1,2:T(8,128)S(1)}, u32[]{:S(2)}, u32[]{:S(2)}) collective-permute-start(f32[224,10,1]{0,1,2:T(8,128)S(1)} %get-tuple-element.26), channel_id=1, source_target_pairs={{1,0},{2,1},{3,2},{4,3},{5,4},{6,5},{7,6},{9,8},{10,9},{11,10},{12... | collective-permute-start | bytes 26888 | tf_op jit(solution)/shard_map/ppermute | solution.py:22
  63.4 2.0 copy-start.2
  68.3 8.4 %copy-start.13 = (f32[224,8,256]{0,1,2:T(8,128)S(1)}, f32[224,8,256]{0,1,2:T(8,128)}, u32[]{:S(2)}) copy-start(f32[224,8,256]{0,1,2:T(8,128)} %copy-done.11) | copy-start | bytes 5505028
  80.6 1.4 copy-start.8
  82.4 7.5 %collective-permute-start.9 = (f32[224,1,256]{2,0,1:T(8,128)S(1)}, f32[224,1,256]{2,0,1:T(8,128)S(1)}, u32[]{:S(2)}, u32[]{:S(2)}) collective-permute-start(f32[224,1,256]{2,0,1:T(8,128)S(1)} %copy.195), channel_id=1, source_target_pairs={{8,0},{16,8},{24,16},{9,1},{17,9},{25,17},{10,2},{18,10},{26,18},{... | collective-permute-start | bytes 688136 | tf_op jit(solution)/shard_map/ppermute | solution.py:22
  83.8 7.7 %collective-permute-start.8 = (f32[224,1,256]{2,0,1:T(8,128)S(1)}, f32[224,1,256]{2,0,1:T(8,128)S(1)}, u32[]{:S(2)}, u32[]{:S(2)}) collective-permute-start(f32[224,1,256]{2,0,1:T(8,128)S(1)} %copy.194), channel_id=1, source_target_pairs={{0,8},{8,16},{16,24},{1,9},{9,17},{17,25},{2,10},{10,18},{18,26},{... | collective-permute-start | bytes 688136 | tf_op jit(solution)/shard_map/ppermute | solution.py:20
  91.7 12.5 %copy-start.9 = (f32[224,8,256]{0,1,2:T(8,128)S(1)}, f32[224,8,256]{0,1,2:T(8,128)}, u32[]{:S(2)}) copy-start(f32[224,8,256]{0,1,2:T(8,128)} %copy-done.8) | copy-start | bytes 5505028
  92.6 7.2 %collective-permute-start.11 = (f32[224,10,1]{0,1,2:T(8,128)S(1)}, f32[224,10,1]{0,1,2:T(8,128)S(1)}, u32[]{:S(2)}, u32[]{:S(2)}) collective-permute-start(f32[224,10,1]{0,1,2:T(8,128)S(1)} %get-tuple-element.25), channel_id=1, source_target_pairs={{0,1},{1,2},{2,3},{3,4},{4,5},{5,6},{6,7},{8,9},{9,10},{10,11},{11... | collective-permute-start | bytes 26888 | tf_op jit(solution)/shard_map/ppermute | solution.py:20
  97.8 5.1 %collective-permute-start.10 = (f32[224,10,1]{0,1,2:T(8,128)S(1)}, f32[224,10,1]{0,1,2:T(8,128)S(1)}, u32[]{:S(2)}, u32[]{:S(2)}) collective-permute-start(f32[224,10,1]{0,1,2:T(8,128)S(1)} %get-tuple-element.24), channel_id=1, source_target_pairs={{1,0},{2,1},{3,2},{4,3},{5,4},{6,5},{7,6},{9,8},{10,9},{11,10},{12... | collective-permute-start | bytes 26888 | tf_op jit(solution)/shard_map/ppermute | solution.py:22
  102.2 2.0 copy-start.3
  107.1 8.4 %copy-start.10 = (f32[224,8,256]{0,1,2:T(8,128)S(1)}, f32[224,8,256]{0,1,2:T(8,128)}, u32[]{:S(2)}) copy-start(f32[224,8,256]{0,1,2:T(8,128)} %copy-done.8) | copy-start | bytes 5505028
  119.4 1.4 copy-start.5
  121.2 7.5 %collective-permute-start.13 = (f32[224,1,256]{2,0,1:T(8,128)S(1)}, f32[224,1,256]{2,0,1:T(8,128)S(1)}, u32[]{:S(2)}, u32[]{:S(2)}) collective-permute-start(f32[224,1,256]{2,0,1:T(8,128)S(1)} %copy.202), channel_id=1, source_target_pairs={{8,0},{16,8},{24,16},{9,1},{17,9},{25,17},{10,2},{18,10},{26,18},{... | collective-permute-start | bytes 688136 | tf_op jit(solution)/shard_map/ppermute | solution.py:22
  122.6 7.7 %collective-permute-start.12 = (f32[224,1,256]{2,0,1:T(8,128)S(1)}, f32[224,1,256]{2,0,1:T(8,128)S(1)}, u32[]{:S(2)}, u32[]{:S(2)}) collective-permute-start(f32[224,1,256]{2,0,1:T(8,128)S(1)} %copy.201), channel_id=1, source_target_pairs={{0,8},{8,16},{16,24},{1,9},{9,17},{17,25},{2,10},{10,18},{18,26},{... | collective-permute-start | bytes 688136 | tf_op jit(solution)/shard_map/ppermute | solution.py:20
  130.5 12.6 %copy-start.6 = (f32[224,8,256]{0,1,2:T(8,128)S(1)}, f32[224,8,256]{0,1,2:T(8,128)}, u32[]{:S(2)}) copy-start(f32[224,8,256]{0,1,2:T(8,128)} %copy-done.5) | copy-start | bytes 5505028
  131.4 7.3 %collective-permute-start.15 = (f32[224,10,1]{0,1,2:T(8,128)S(1)}, f32[224,10,1]{0,1,2:T(8,128)S(1)}, u32[]{:S(2)}, u32[]{:S(2)}) collective-permute-start(f32[224,10,1]{0,1,2:T(8,128)S(1)} %get-tuple-element.23), channel_id=1, source_target_pairs={{0,1},{1,2},{2,3},{3,4},{4,5},{5,6},{6,7},{8,9},{9,10},{10,11},{11... | collective-permute-start | bytes 26888 | tf_op jit(solution)/shard_map/ppermute | solution.py:20
  136.8 5.1 %collective-permute-start.14 = (f32[224,10,1]{0,1,2:T(8,128)S(1)}, f32[224,10,1]{0,1,2:T(8,128)S(1)}, u32[]{:S(2)}, u32[]{:S(2)}) collective-permute-start(f32[224,10,1]{0,1,2:T(8,128)S(1)} %get-tuple-element.22), channel_id=1, source_target_pairs={{1,0},{2,1},{3,2},{4,3},{5,4},{6,5},{7,6},{9,8},{10,9},{11,10},{12... | collective-permute-start | bytes 26888 | tf_op jit(solution)/shard_map/ppermute | solution.py:22
  141.1 2.0 copy-start.4
  146.1 8.4 %copy-start.7 = (f32[224,8,256]{0,1,2:T(8,128)S(1)}, f32[224,8,256]{0,1,2:T(8,128)}, u32[]{:S(2)}) copy-start(f32[224,8,256]{0,1,2:T(8,128)} %copy-done.5) | copy-start | bytes 5505028
  158.3 1.3 copy-start.14
  167.3 149.2 %copy-start.15 = (f32[224,8,256]{2,1,0:T(8,128)}, f32[224,8,256]{2,1,0:T(8,128)S(1)}, u32[]{:S(2)}) copy-start(f32[224,8,256]{2,1,0:T(8,128)S(1)} %copy.215) | copy-start | bytes 5505028
Sparse Core Ops, SparseCore 0:
  164.8 126.7 all-reduce.1
where the time goes:
time: 326 us; the launch traced here: 325 us
  waiting for transfers between devices  137 us (42%)
  other arithmetic  82.5 us (25%)
  starting transfers between devices  53.1 us (16%)
  local copies, waits for them, and re-layouts  24.8 us (8%)
  between operations  14.7 us (5%)
  matrix products  13 us (4%)
    psum x1, waiting for transfers between devices, shards(): gram_full = lax.psum(local_gram, ('row', 'col'))  122 us
    ppermute x8, starting transfers between devices, padded_2(): lax.ppermute(tail, axis, [(i, (i + 1) % count) for i in range(ends)])  40 us
    mul x4, other arithmetic, smooth_step(): flux_col = weight * diff_col  31.7 us
    unnamed x38, local copies, waits for them, and re-layouts  18.3 us
    ppermute x8, starting transfers between devices, padded_2(): lax.ppermute(head, axis, [((i + 1) % count, i) for i in range(ends)])  13 us
    add x4, other arithmetic, smooth_step(): return centre + tau_step * spread + tau_step * fidelity * (source - centre)  12.4 us
    reduce_sum x4, other arithmetic, smooth_step(): energy_sum = jnp.sum(diff_col * diff_col + diff_row * diff_row, axis=0)  11 us
    ppermute x8, waiting for transfers between devices, padded_2(): lax.ppermute(head, axis, [((i + 1) % count, i) for i in range(ends)])  9.65 us
  transfers between devices with their start and end apart: 17, of which 13 were waited for; matrix products, arithmetic and copies ran while one was open for 5% of the time, Pallas kernels for 0%

commit v1 on v0

--- a/solution.py
+++ b/solution.py
@@ -69,7 +69,7 @@
         precision=lax.Precision.HIGHEST,
         preferred_element_type=jnp.float32,
     )
-    gram_full = lax.psum(local_gram, ("row", "col"))
+    gram_full = jnp.sum(lax.all_gather(local_gram, ("row", "col")), axis=0)
     for turn in range(SUBIT):
         product = jnp.dot(gram_full, basis_now, precision=lax.Precision.HIGHEST)
         basis_now = orthonormal(orthonormal(product))

time: 326 us -> 278 us (0.85)
  waiting for transfers between devices: 137 us -> 87 us
  other arithmetic: 82.5 us -> 86.1 us
    psum x1 -> x0, waiting for transfers between devices: 122 us -> none  [shards(): gram_full = lax.psum(local_gram, ('row', 'col'))]
    all_gather x0 -> x1, waiting for transfers between devices: none -> 72 us  [shards(): gram_full = jnp.sum(lax.all_gather(local_gram, ('row', 'col')), axis=0)]
    reduce_sum x0 -> x1, other arithmetic: none -> 3.61 us  [shards(): gram_full = jnp.sum(lax.all_gather(local_gram, ('row', 'col')), axis=0)]
  transfers between devices with their start and end apart: 17 -> 17, of which waited for: 13 -> 13; matrix products, arithmetic and copies ran while one was open for 5% -> 6% of each run, Pallas kernels for 0% -> 0%
where the time goes in v1:
time: 278 us; the launch traced here: 277 us
  waiting for transfers between devices  87 us (31%)
  other arithmetic  86.1 us (31%)
  starting transfers between devices  53.1 us (19%)
  local copies, waits for them, and re-layouts  24.8 us (9%)
  between operations  14.7 us (5%)
  matrix products  11.1 us (4%)
    all_gather x1, waiting for transfers between devices, shards(): gram_full = jnp.sum(lax.all_gather(local_gram, ('row', 'col')), axis=0)  72 us
    ppermute x8, starting transfers between devices, padded_2(): lax.ppermute(tail, axis, [(i, (i + 1) % count) for i in range(ends)])  40 us
    mul x4, other arithmetic, smooth_step(): flux_col = weight * diff_col  31.7 us
    unnamed x38, local copies, waits for them, and re-layouts  18.3 us
    ppermute x8, starting transfers between devices, padded_2(): lax.ppermute(head, axis, [((i + 1) % count, i) for i in range(ends)])  13 us
    add x4, other arithmetic, smooth_step(): return centre + tau_step * spread + tau_step * fidelity * (source - centre)  12.4 us
    reduce_sum x4, other arithmetic, smooth_step(): energy_sum = jnp.sum(diff_col * diff_col + diff_row * diff_row, axis=0)  11 us
    ppermute x8, waiting for transfers between devices, padded_2(): lax.ppermute(head, axis, [((i + 1) % count, i) for i in range(ends)])  9.65 us
  transfers between devices with their start and end apart: 17, of which 13 were waited for; matrix products, arithmetic and copies ran while one was open for 6% of the time, Pallas kernels for 0%

profile of v1, /device:TPU:1, one launch (start us, length us, event | category | flops | bytes accessed | tf_op | source)
XLA Modules:
  0.0 276.8 jit_solution(650038881157199222)
XLA Ops:
  7.2 2.4 fusion.42
  9.6 1.3 collective-permute-start.1
  10.9 4.7 %collective-permute-start = (f32[224,1,256]{2,0,1:T(8,128)S(1)}, f32[224,1,256]{2,0,1:T(8,128)S(1)}, u32[]{:S(2)}, u32[]{:S(2)}) collective-permute-start(f32[224,1,256]{2,0,1:T(8,128)S(1)} %copy.216), channel_id=1, source_target_pairs={{0,8},{8,16},{16,24},{1,9},{9,17},{17,25},{2,10},{10,18},{18,26},{... | collective-permute-start | bytes 688136 | tf_op jit(solution)/shard_map/ppermute | solution.py:20
  15.6 2.2 copy.184
  17.9 1.1 collective-permute-done.1
  20.0 4.7 %collective-permute-start.3 = (f32[224,10,1]{0,1,2:T(8,128)S(1)}, f32[224,10,1]{0,1,2:T(8,128)S(1)}, u32[]{:S(2)}, u32[]{:S(2)}) collective-permute-start(f32[224,10,1]{0,1,2:T(8,128)S(1)} %get-tuple-element.29), channel_id=1, source_target_pairs={{0,1},{1,2},{2,3},{3,4},{4,5},{5,6},{6,7},{8,9},{9,10},{10,11},{11... | collective-permute-start | bytes 26888 | tf_op jit(solution)/shard_map/ppermute | solution.py:20
  24.8 1.9 collective-permute-start.2
  27.6 2.3 collective-permute-done.2
  29.8 2.7 add_reduce_fusion.3
  32.8 6.5 %broadcast_multiply_fusion.7 = (f32[224,9,257]{0,1,2:T(8,128)S(1)}, f32[224,9,257]{0,1,2:T(8,128)S(1)}) fusion(f32[9,257]{0,1:T(8,128)S(1)} %copy.183, f32[224,10,257]{0,1,2:T(8,128)} %copy-done.1, f32[224,10,1]{0,1,2:T(8,128)S(1)} %collective-permute-done.2, f32[224,1,256]{0,1,2:T(1,128)S(1)} %copy.181, f32[224,8,256]{0,1,2:T(8,128)S(1)} %copy.184, ...), kind=kLoop, calls=%fused_computation.35 | loop fusion | flops 3626784 | bytes 10601764 | tf_op jit(solution)/shard_map/mul | solution.py:39
  39.4 1.0 fusion.15
  40.3 1.3 copy-done.11
  42.1 1.3 collective-permute-start.5
  43.6 4.7 %collective-permute-start.4 = (f32[224,1,256]{2,0,1:T(8,128)S(1)}, f32[224,1,256]{2,0,1:T(8,128)S(1)}, u32[]{:S(2)}, u32[]{:S(2)}) collective-permute-start(f32[224,1,256]{2,0,1:T(8,128)S(1)} %copy.187), channel_id=1, source_target_pairs={{0,8},{8,16},{16,24},{1,9},{9,17},{17,25},{2,10},{10,18},{18,26},{... | collective-permute-start | bytes 688136 | tf_op jit(solution)/shard_map/ppermute | solution.py:20
  48.3 2.0 collective-permute-done.5
  50.5 1.7 collective-permute-done.4
  53.3 5.5 %collective-permute-start.7 = (f32[224,10,1]{0,1,2:T(8,128)S(1)}, f32[224,10,1]{0,1,2:T(8,128)S(1)}, u32[]{:S(2)}, u32[]{:S(2)}) collective-permute-start(f32[224,10,1]{0,1,2:T(8,128)S(1)} %get-tuple-element.27), channel_id=1, source_target_pairs={{0,1},{1,2},{2,3},{3,4},{4,5},{5,6},{6,7},{8,9},{9,10},{10,11},{11... | collective-permute-start | bytes 26888 | tf_op jit(solution)/shard_map/ppermute | solution.py:20
  58.8 2.1 collective-permute-start.6
  60.9 2.4 maximum_maximum_fusion.1
  63.9 1.5 copy-done.2
  65.3 2.8 add_reduce_fusion.2
  68.4 8.4 %broadcast_multiply_fusion.5 = (f32[224,9,257]{0,1,2:T(8,128)S(1)}, f32[224,9,257]{0,1,2:T(8,128)}) fusion(f32[9,257]{0,1:T(8,128)S(1)} %copy.192, f32[224,10,257]{0,1,2:T(8,128)} %copy-done.2, f32[224,10,1]{0,1,2:T(8,128)S(1)} %collective-permute-done.6, f32[224,1,256]{0,1,2:T(1,128)S(1)} %copy.190, f32[224,8,256]{0,1,2:T(8,128)} %copy-done.11, ...), kind=kLoop, calls=%fused_computation.33 | loop fusion | flops 3626784 | bytes 10601764 | tf_op jit(solution)/shard_map/mul | solution.py:39
  76.7 3.8 %fusion.12 = f32[224,8,256]{0,1,2:T(8,128)S(1)} fusion(f32[224,8,256]{0,1,2:T(8,128)S(1)} %copy-done.13, f32[224,9,257]{0,1,2:T(8,128)} %get-tuple-element.19, f32[224,9,257]{0,1,2:T(8,128)S(1)} %get-tuple-element.18, f32[224,8,256]{0,1,2:T(8,128)S(1)} %copy.184), kind=kLoop, calls=%fused_computation.51 | loop fusion | flops 3670016 | bytes 12845056 | tf_op jit(solution)/shard_map/add | solution.py:48
  80.6 1.3 copy-done.8
  82.4 1.3 collective-permute-start.9
  83.8 4.7 %collective-permute-start.8 = (f32[224,1,256]{2,0,1:T(8,128)S(1)}, f32[224,1,256]{2,0,1:T(8,128)S(1)}, u32[]{:S(2)}, u32[]{:S(2)}) collective-permute-start(f32[224,1,256]{2,0,1:T(8,128)S(1)} %copy.194), channel_id=1, source_target_pairs={{0,8},{8,16},{16,24},{1,9},{9,17},{17,25},{2,10},{10,18},{18,26},{... | collective-permute-start | bytes 688136 | tf_op jit(solution)/shard_map/ppermute | solution.py:20
  88.6 1.3 collective-permute-done.9
  90.1 1.5 collective-permute-done.8
  92.6 5.2 %collective-permute-start.11 = (f32[224,10,1]{0,1,2:T(8,128)S(1)}, f32[224,10,1]{0,1,2:T(8,128)S(1)}, u32[]{:S(2)}, u32[]{:S(2)}) collective-permute-start(f32[224,10,1]{0,1,2:T(8,128)S(1)} %get-tuple-element.25), channel_id=1, source_target_pairs={{0,1},{1,2},{2,3},{3,4},{4,5},{5,6},{6,7},{8,9},{9,10},{10,11},{11... | collective-permute-start | bytes 26888 | tf_op jit(solution)/shard_map/ppermute | solution.py:20
  97.8 1.9 collective-permute-start.10
  99.7 2.4 maximum_maximum_fusion.2
  102.9 1.3 copy-done.3
  104.1 2.8 add_reduce_fusion.1
  107.2 8.4 %broadcast_multiply_fusion.3 = (f32[224,9,257]{0,1,2:T(8,128)S(1)}, f32[224,9,257]{0,1,2:T(8,128)}) fusion(f32[9,257]{0,1:T(8,128)S(1)} %copy.199, f32[224,10,257]{0,1,2:T(8,128)} %copy-done.3, f32[224,10,1]{0,1,2:T(8,128)S(1)} %collective-permute-done.10, f32[224,1,256]{0,1,2:T(1,128)S(1)} %copy.197, f32[224,8,256]{0,1,2:T(8,128)} %copy-done.8, ...), kind=kLoop, calls=%fused_computation.31 | loop fusion | flops 3626784 | bytes 10601764 | tf_op jit(solution)/shard_map/mul | solution.py:39
  115.5 3.8 %fusion.9 = f32[224,8,256]{0,1,2:T(8,128)S(1)} fusion(f32[224,8,256]{0,1,2:T(8,128)S(1)} %copy-done.10, f32[224,9,257]{0,1,2:T(8,128)} %get-tuple-element.17, f32[224,9,257]{0,1,2:T(8,128)S(1)} %get-tuple-element.16, f32[224,8,256]{0,1,2:T(8,128)S(1)} %copy.184), kind=kLoop, calls=%fused_computation.45 | loop fusion | flops 3670016 | bytes 12845056 | tf_op jit(solution)/shard_map/add | solution.py:48
  119.4 1.3 copy-done.5
  121.2 1.3 collective-permute-start.13
  122.6 5.0 %collective-permute-start.12 = (f32[224,1,256]{2,0,1:T(8,128)S(1)}, f32[224,1,256]{2,0,1:T(8,128)S(1)}, u32[]{:S(2)}, u32[]{:S(2)}) collective-permute-start(f32[224,1,256]{2,0,1:T(8,128)S(1)} %copy.201), channel_id=1, source_target_pairs={{0,8},{8,16},{16,24},{1,9},{9,17},{17,25},{2,10},{10,18},{18,26},{... | collective-permute-start | bytes 688136 | tf_op jit(solution)/shard_map/ppermute | solution.py:20
  127.6 1.1 collective-permute-done.13
  128.9 1.5 collective-permute-done.12
  131.4 5.4 %collective-permute-start.15 = (f32[224,10,1]{0,1,2:T(8,128)S(1)}, f32[224,10,1]{0,1,2:T(8,128)S(1)}, u32[]{:S(2)}, u32[]{:S(2)}) collective-permute-start(f32[224,10,1]{0,1,2:T(8,128)S(1)} %get-tuple-element.23), channel_id=1, source_target_pairs={{0,1},{1,2},{2,3},{3,4},{4,5},{5,6},{6,7},{8,9},{9,10},{10,11},{11... | collective-permute-start | bytes 26888 | tf_op jit(solution)/shard_map/ppermute | solution.py:20
  136.8 1.9 collective-permute-start.14
  138.7 2.4 maximum_maximum_fusion.3
  141.8 1.3 copy-done.4
  143.1 2.8 add_reduce_fusion
  146.1 8.4 %broadcast_multiply_fusion.1 = (f32[224,9,257]{0,1,2:T(8,128)S(1)}, f32[224,9,257]{0,1,2:T(8,128)}) fusion(f32[9,257]{0,1:T(8,128)S(1)} %copy.206, f32[224,10,257]{0,1,2:T(8,128)} %copy-done.4, f32[224,10,1]{0,1,2:T(8,128)S(1)} %collective-permute-done.14, f32[224,1,256]{0,1,2:T(1,128)S(1)} %copy.204, f32[224,8,256]{0,1,2:T(8,128)} %copy-done.5, ...), kind=kLoop, calls=%fused_computation.29 | loop fusion | flops 3626784 | bytes 10601764 | tf_op jit(solution)/shard_map/mul | solution.py:39
  154.5 3.8 %fusion.6 = f32[224,8,256]{0,1,2:T(8,128)S(1)} fusion(f32[224,8,256]{0,1,2:T(8,128)S(1)} %copy-done.7, f32[224,9,257]{0,1,2:T(8,128)} %get-tuple-element.15, f32[224,9,257]{0,1,2:T(8,128)S(1)} %get-tuple-element.14, f32[224,8,256]{0,1,2:T(8,128)S(1)} %copy.184), kind=kLoop, calls=%fused_computation.39 | loop fusion | flops 3670016 | bytes 12845056 | tf_op jit(solution)/shard_map/add | solution.py:48
  158.3 1.4 copy-done.14
  159.7 5.0 %fusion.18 = f32[224,224]{1,0:T(8,128)} fusion(f32[224,8,256]{0,1,2:T(8,128)S(1)} %fusion.6), kind=kOutput, calls=%fused_computation.62 | convolution fusion | flops 1233125376 | bytes 2035712 | tf_op jit(solution)/shard_map/dot_general | solution.py:65
  164.8 2.6 copy.215
  167.4 2.0 copy.218
  169.3 72.0 %all-gather.3.cloned.1.call-done = f32[7168,224]{1,0:T(8,128)} async-done(((f32[224,224]{1,0:T(8,128)}), f32[7168,224]{1,0:T(8,128)}) %all-gather.3.cloned.1.call-update) | async-done | bytes 6422544 | tf_op jit(solution)/shard_map/all_gather | solution.py:72
  241.4 3.6 %reduce_sum.49 = f32[224,224]{1,0:T(8,128)S(1)} reduce(f32[32,224,224]{2,1,0:T(8,128)} %bitcast.74, f32[]{:T(128)} %constant.38.clone.1), dimensions={0}, to_apply=%region_4.0 | reduce | flops 1555456 | bytes 6623236 | tf_op jit(solution)/shard_map/reduce_sum | solution.py:72
  245.5 1.5 cholesky.74
  248.4 1.2 custom-call.8
  250.1 1.5 cholesky.85
  253.0 1.2 custom-call.9
  255.0 1.5 cholesky.96
  257.9 1.2 custom-call.10
  259.5 1.5 cholesky.107
  262.4 1.2 custom-call.11
  263.9 2.5 fusion.49
  266.4 1.6 fusion.50
  268.0 2.0 copy.219
  (101 shorter events, 18.2 us)
Async XLA Ops:
  7.2 237.8 %copy-start = (f32[224,16]{0,1:T(8,128)S(1)}, f32[224,16]{0,1:T(8,128)}, u32[]{:S(2)}) copy-start(f32[224,16]{0,1:T(8,128)} %param.6) | copy-start | bytes 43012
  7.2 234.2 %all-gather.3.cloned.1.call-start = ((), (), s32[]{:S(2)}) async-start(), calls=%async_computation | async-start | bytes 7569408 | tf_op jit(solution)/shard_map/all_gather | solution.py:72
  9.6 9.4 %collective-permute-start.1 = (f32[224,1,256]{2,0,1:T(8,128)S(1)}, f32[224,1,256]{2,0,1:T(8,128)S(1)}, u32[]{:S(2)}, u32[]{:S(2)}) collective-permute-start(f32[224,1,256]{2,0,1:T(8,128)S(1)} %copy.217), channel_id=1, source_target_pairs={{8,0},{16,8},{24,16},{9,1},{17,9},{25,17},{10,2},{18,10},{26,18},{... | collective-permute-start | bytes 688136 | tf_op jit(solution)/shard_map/ppermute | solution.py:22
  10.9 8.9 %collective-permute-start = (f32[224,1,256]{2,0,1:T(8,128)S(1)}, f32[224,1,256]{2,0,1:T(8,128)S(1)}, u32[]{:S(2)}, u32[]{:S(2)}) collective-permute-start(f32[224,1,256]{2,0,1:T(8,128)S(1)} %copy.216), channel_id=1, source_target_pairs={{0,8},{8,16},{16,24},{1,9},{9,17},{17,25},{2,10},{10,18},{18,26},{... | collective-permute-start | bytes 688136 | tf_op jit(solution)/shard_map/ppermute | solution.py:20
  20.0 6.6 %collective-permute-start.3 = (f32[224,10,1]{0,1,2:T(8,128)S(1)}, f32[224,10,1]{0,1,2:T(8,128)S(1)}, u32[]{:S(2)}, u32[]{:S(2)}) collective-permute-start(f32[224,10,1]{0,1,2:T(8,128)S(1)} %get-tuple-element.29), channel_id=1, source_target_pairs={{0,1},{1,2},{2,3},{3,4},{4,5},{5,6},{6,7},{8,9},{9,10},{10,11},{11... | collective-permute-start | bytes 26888 | tf_op jit(solution)/shard_map/ppermute | solution.py:20
  24.8 5.1 %collective-permute-start.2 = (f32[224,10,1]{0,1,2:T(8,128)S(1)}, f32[224,10,1]{0,1,2:T(8,128)S(1)}, u32[]{:S(2)}, u32[]{:S(2)}) collective-permute-start(f32[224,10,1]{0,1,2:T(8,128)S(1)} %get-tuple-element.28), channel_id=1, source_target_pairs={{1,0},{2,1},{3,2},{4,3},{5,4},{6,5},{7,6},{9,8},{10,9},{11,10},{12... | collective-permute-start | bytes 26888 | tf_op jit(solution)/shard_map/ppermute | solution.py:22
  27.5 2.3 copy-start.1
  40.3 1.4 copy-start.11
  42.1 8.2 %collective-permute-start.5 = (f32[224,1,256]{2,0,1:T(8,128)S(1)}, f32[224,1,256]{2,0,1:T(8,128)S(1)}, u32[]{:S(2)}, u32[]{:S(2)}) collective-permute-start(f32[224,1,256]{2,0,1:T(8,128)S(1)} %copy.188), channel_id=1, source_target_pairs={{8,0},{16,8},{24,16},{9,1},{17,9},{25,17},{10,2},{18,10},{26,18},{... | collective-permute-start | bytes 688136 | tf_op jit(solution)/shard_map/ppermute | solution.py:22
  43.6 8.6 %collective-permute-start.4 = (f32[224,1,256]{2,0,1:T(8,128)S(1)}, f32[224,1,256]{2,0,1:T(8,128)S(1)}, u32[]{:S(2)}, u32[]{:S(2)}) collective-permute-start(f32[224,1,256]{2,0,1:T(8,128)S(1)} %copy.187), channel_id=1, source_target_pairs={{0,8},{8,16},{16,24},{1,9},{9,17},{17,25},{2,10},{10,18},{18,26},{... | collective-permute-start | bytes 688136 | tf_op jit(solution)/shard_map/ppermute | solution.py:20
  52.4 13.0 %copy-start.12 = (f32[224,8,256]{0,1,2:T(8,128)S(1)}, f32[224,8,256]{0,1,2:T(8,128)}, u32[]{:S(2)}) copy-start(f32[224,8,256]{0,1,2:T(8,128)} %copy-done.11) | copy-start | bytes 5505028
  53.3 7.7 %collective-permute-start.7 = (f32[224,10,1]{0,1,2:T(8,128)S(1)}, f32[224,10,1]{0,1,2:T(8,128)S(1)}, u32[]{:S(2)}, u32[]{:S(2)}) collective-permute-start(f32[224,10,1]{0,1,2:T(8,128)S(1)} %get-tuple-element.27), channel_id=1, source_target_pairs={{0,1},{1,2},{2,3},{3,4},{4,5},{5,6},{6,7},{8,9},{9,10},{10,11},{11... | collective-permute-start | bytes 26888 | tf_op jit(solution)/shard_map/ppermute | solution.py:20
  58.8 5.1 %collective-permute-start.6 = (f32[224,10,1]{0,1,2:T(8,128)S(1)}, f32[224,10,1]{0,1,2:T(8,128)S(1)}, u32[]{:S(2)}, u32[]{:S(2)}) collective-permute-start(f32[224,10,1]{0,1,2:T(8,128)S(1)} %get-tuple-element.26), channel_id=1, source_target_pairs={{1,0},{2,1},{3,2},{4,3},{5,4},{6,5},{7,6},{9,8},{10,9},{11,10},{12... | collective-permute-start | bytes 26888 | tf_op jit(solution)/shard_map/ppermute | solution.py:22
  63.4 2.0 copy-start.2
  68.3 8.4 %copy-start.13 = (f32[224,8,256]{0,1,2:T(8,128)S(1)}, f32[224,8,256]{0,1,2:T(8,128)}, u32[]{:S(2)}) copy-start(f32[224,8,256]{0,1,2:T(8,128)} %copy-done.11) | copy-start | bytes 5505028
  80.6 1.4 copy-start.8
  82.4 7.5 %collective-permute-start.9 = (f32[224,1,256]{2,0,1:T(8,128)S(1)}, f32[224,1,256]{2,0,1:T(8,128)S(1)}, u32[]{:S(2)}, u32[]{:S(2)}) collective-permute-start(f32[224,1,256]{2,0,1:T(8,128)S(1)} %copy.195), channel_id=1, source_target_pairs={{8,0},{16,8},{24,16},{9,1},{17,9},{25,17},{10,2},{18,10},{26,18},{... | collective-permute-start | bytes 688136 | tf_op jit(solution)/shard_map/ppermute | solution.py:22
  83.8 7.7 %collective-permute-start.8 = (f32[224,1,256]{2,0,1:T(8,128)S(1)}, f32[224,1,256]{2,0,1:T(8,128)S(1)}, u32[]{:S(2)}, u32[]{:S(2)}) collective-permute-start(f32[224,1,256]{2,0,1:T(8,128)S(1)} %copy.194), channel_id=1, source_target_pairs={{0,8},{8,16},{16,24},{1,9},{9,17},{17,25},{2,10},{10,18},{18,26},{... | collective-permute-start | bytes 688136 | tf_op jit(solution)/shard_map/ppermute | solution.py:20
  91.7 12.5 %copy-start.9 = (f32[224,8,256]{0,1,2:T(8,128)S(1)}, f32[224,8,256]{0,1,2:T(8,128)}, u32[]{:S(2)}) copy-start(f32[224,8,256]{0,1,2:T(8,128)} %copy-done.8) | copy-start | bytes 5505028
  92.6 7.2 %collective-permute-start.11 = (f32[224,10,1]{0,1,2:T(8,128)S(1)}, f32[224,10,1]{0,1,2:T(8,128)S(1)}, u32[]{:S(2)}, u32[]{:S(2)}) collective-permute-start(f32[224,10,1]{0,1,2:T(8,128)S(1)} %get-tuple-element.25), channel_id=1, source_target_pairs={{0,1},{1,2},{2,3},{3,4},{4,5},{5,6},{6,7},{8,9},{9,10},{10,11},{11... | collective-permute-start | bytes 26888 | tf_op jit(solution)/shard_map/ppermute | solution.py:20
  97.8 5.1 %collective-permute-start.10 = (f32[224,10,1]{0,1,2:T(8,128)S(1)}, f32[224,10,1]{0,1,2:T(8,128)S(1)}, u32[]{:S(2)}, u32[]{:S(2)}) collective-permute-start(f32[224,10,1]{0,1,2:T(8,128)S(1)} %get-tuple-element.24), channel_id=1, source_target_pairs={{1,0},{2,1},{3,2},{4,3},{5,4},{6,5},{7,6},{9,8},{10,9},{11,10},{12... | collective-permute-start | bytes 26888 | tf_op jit(solution)/shard_map/ppermute | solution.py:22
  102.2 2.0 copy-start.3
  107.1 8.4 %copy-start.10 = (f32[224,8,256]{0,1,2:T(8,128)S(1)}, f32[224,8,256]{0,1,2:T(8,128)}, u32[]{:S(2)}) copy-start(f32[224,8,256]{0,1,2:T(8,128)} %copy-done.8) | copy-start | bytes 5505028
  119.4 1.4 copy-start.5
  121.2 7.5 %collective-permute-start.13 = (f32[224,1,256]{2,0,1:T(8,128)S(1)}, f32[224,1,256]{2,0,1:T(8,128)S(1)}, u32[]{:S(2)}, u32[]{:S(2)}) collective-permute-start(f32[224,1,256]{2,0,1:T(8,128)S(1)} %copy.202), channel_id=1, source_target_pairs={{8,0},{16,8},{24,16},{9,1},{17,9},{25,17},{10,2},{18,10},{26,18},{... | collective-permute-start | bytes 688136 | tf_op jit(solution)/shard_map/ppermute | solution.py:22
  122.6 7.7 %collective-permute-start.12 = (f32[224,1,256]{2,0,1:T(8,128)S(1)}, f32[224,1,256]{2,0,1:T(8,128)S(1)}, u32[]{:S(2)}, u32[]{:S(2)}) collective-permute-start(f32[224,1,256]{2,0,1:T(8,128)S(1)} %copy.201), channel_id=1, source_target_pairs={{0,8},{8,16},{16,24},{1,9},{9,17},{17,25},{2,10},{10,18},{18,26},{... | collective-permute-start | bytes 688136 | tf_op jit(solution)/shard_map/ppermute | solution.py:20
  130.5 12.6 %copy-start.6 = (f32[224,8,256]{0,1,2:T(8,128)S(1)}, f32[224,8,256]{0,1,2:T(8,128)}, u32[]{:S(2)}) copy-start(f32[224,8,256]{0,1,2:T(8,128)} %copy-done.5) | copy-start | bytes 5505028
  131.4 7.3 %collective-permute-start.15 = (f32[224,10,1]{0,1,2:T(8,128)S(1)}, f32[224,10,1]{0,1,2:T(8,128)S(1)}, u32[]{:S(2)}, u32[]{:S(2)}) collective-permute-start(f32[224,10,1]{0,1,2:T(8,128)S(1)} %get-tuple-element.23), channel_id=1, source_target_pairs={{0,1},{1,2},{2,3},{3,4},{4,5},{5,6},{6,7},{8,9},{9,10},{10,11},{11... | collective-permute-start | bytes 26888 | tf_op jit(solution)/shard_map/ppermute | solution.py:20
  136.8 5.1 %collective-permute-start.14 = (f32[224,10,1]{0,1,2:T(8,128)S(1)}, f32[224,10,1]{0,1,2:T(8,128)S(1)}, u32[]{:S(2)}, u32[]{:S(2)}) collective-permute-start(f32[224,10,1]{0,1,2:T(8,128)S(1)} %get-tuple-element.22), channel_id=1, source_target_pairs={{1,0},{2,1},{3,2},{4,3},{5,4},{6,5},{7,6},{9,8},{10,9},{11,10},{12... | collective-permute-start | bytes 26888 | tf_op jit(solution)/shard_map/ppermute | solution.py:22
  141.1 2.0 copy-start.4
  146.1 8.4 %copy-start.7 = (f32[224,8,256]{0,1,2:T(8,128)S(1)}, f32[224,8,256]{0,1,2:T(8,128)}, u32[]{:S(2)}) copy-start(f32[224,8,256]{0,1,2:T(8,128)} %copy-done.5) | copy-start | bytes 5505028
  158.3 1.4 copy-start.14
  167.4 77.6 %copy-start.15 = (f32[224,8,256]{2,1,0:T(8,128)}, f32[224,8,256]{2,1,0:T(8,128)S(1)}, u32[]{:S(2)}) copy-start(f32[224,8,256]{2,1,0:T(8,128)S(1)} %copy.215) | copy-start | bytes 5505028
Sparse Core Ops, SparseCore 0:
  164.9 76.4 all-gather.2
